TPU v7x, 32 devices: a whole 2x2x4 slice. The times are simulated.
32 devices in a mesh: tm: 4 (over y, x), series: 8 (over z, core).
Axes of the slice: x: 2, y: 2, z: 4, core: 2. Of those that a mesh axis runs over, the one named last changes fastest.
Arguments:
- codes: int32 [8, 512], P(None, ('tm', 'series')), may hold values from 0 to 916478, as said below
- owner_slot: int32 [8], replicated, may hold values from 0 to 7, each once
- edges: int32 [4096], replicated, may hold values from 0 to 2096640, as said below
- w_in: bfloat16 [128, 2304], replicated, may hold values from -0.09375 to 0.09375
- w_dt: bfloat16 [128, 32], replicated, may hold values from -0.5 to 0.5
- dt_bias: float32 [32], replicated, may hold values from -1 to 1
- decay_rate: float32 [32], replicated, may hold values from 1e-05 to 0.1
- grad_out: bfloat16 [8, 512, 2048], P('series', 'tm'), may hold values from -6 to 6
Outputs:
- ssd_output: bfloat16 [8, 512, 2048], P('series', 'tm')
- grad_in: float32 [128, 2304], replicated
Inputs may be any that keep to these rules, and one draw needn't show every extreme that they name: `codes`: each row is one series in the order of ingestion slots. edges[0] is 0 and edges rise strictly.
All inputs are finite; a program needn't handle non-finite values.
Results may differ from a plain program's by a relative error of at most 0.0062.
The roundings to bfloat16 on the way count: a program that leaves them out, or rounds other values in their place, can miss the bound.
Values sent between devices are 32-bit elements; how exact they have to be, the bound alone decides.
No kernel may reach another device: no remote copies, remote signals or barrier semaphores. Data moves between devices by JAX's collectives and lax.ppermute only.
A program may use at most 128 MiB of HBM per device.

v0:
```python
import math
import jax
import jax.numpy as jnp
from jax import lax
from jax.sharding import PartitionSpec as P

code_ceiling = 2097152.0


def decay_matrix(cum_decay):
    row_count = cum_decay.shape[0]
    causal = jnp.arange(row_count)[:, None] >= jnp.arange(row_count)[None, :]
    log_span = cum_decay.T[:, :, None] - cum_decay.T[:, None, :]
    return jnp.where(causal[None], jnp.exp(jnp.where(causal[None], log_span, -60.0)), 0.0)


def on_device(codes, owner_slot, edges, w_in, w_dt, dt_bias, decay_rate, grad_out):
    fl = jnp.float32
    half = jnp.bfloat16
    tok_rows = grad_out.shape[1]
    head_count = dt_bias.shape[0]
    inner_width = grad_out.shape[2]
    head_dim = inner_width // head_count
    state_dim = (w_in.shape[1] - inner_width) // 2
    n_blocks = lax.axis_size("tm")
    seq_len = tok_rows * n_blocks
    series_count = lax.axis_size("series")
    my_block = lax.axis_index("tm")
    my_series = lax.axis_index("series")
    all_codes = lax.all_gather(codes, ("tm", "series"), axis=1, tiled=True)
    row = lax.dynamic_index_in_dim(all_codes, owner_slot[my_series], axis=0, keepdims=False)
    reading = row.astype(fl)
    edge_float = edges.astype(fl)
    upper_edge = jnp.concatenate([edge_float[1:], jnp.full((1,), code_ceiling, fl)])
    onehot = (
        (edge_float[None, :] <= reading[:, None]) & (upper_edge[None, :] > reading[:, None])
    ).astype(fl)
    counts = jnp.sum(onehot, axis=0)
    before = jnp.cumsum(counts) - counts
    bin_table = jnp.stack([before, counts, edge_float, upper_edge - edge_float], axis=1)
    picked = jnp.dot(onehot, bin_table, precision=lax.Precision.HIGHEST)
    within_bin = (reading - picked[:, 2]) / picked[:, 3]
    quantile = (picked[:, 0] + picked[:, 1] * within_bin) / seq_len
    frequency = (jnp.arange(w_in.shape[0], dtype=fl) + 0.5) * math.pi
    features_all = jnp.cos(quantile[:, None] * frequency).astype(half)
    projected_all = jnp.dot(features_all, w_in, preferred_element_type=fl).astype(half)
    projected_all = projected_all.reshape(n_blocks, tok_rows, -1)
    x_all = projected_all[:, :, :inner_width].reshape(n_blocks, tok_rows, head_count, head_dim)
    b_all = projected_all[:, :, inner_width : inner_width + state_dim]
    c_all = projected_all[:, :, inner_width + state_dim :]
    step_all = jax.nn.softplus(
        dt_bias + jnp.dot(features_all, w_dt, preferred_element_type=fl)
    ).reshape(n_blocks, tok_rows, head_count)
    cum_all = jnp.cumsum(-step_all * decay_rate, axis=1)
    gate_all = jnp.exp(cum_all[:, -1])
    tail_all = jnp.exp(cum_all[:, -1:, :] - cum_all) * step_all
    xw_all = (x_all * tail_all[..., None]).astype(half)
    state_local_all = jnp.einsum("bthp,btn->bhpn", xw_all, b_all, preferred_element_type=fl)
    state_in = jnp.zeros((head_count, head_dim, state_dim), fl)
    for k in range(n_blocks - 1):
        new = gate_all[k][:, None, None] * state_in + state_local_all[k]
        state_in = jnp.where(k < my_block, new, state_in)

    def mine(a):
        return lax.dynamic_index_in_dim(a, my_block, axis=0, keepdims=False)

    features = mine(features_all.reshape(n_blocks, tok_rows, -1))
    x_heads = mine(x_all)
    b_proj = mine(b_all)
    c_proj = mine(c_all)
    step_size = mine(step_all)
    cum_decay = mine(cum_all)
    tail_factor = mine(tail_all)
    x_weighted = mine(xw_all)
    head_factor = jnp.exp(cum_decay)
    grad_heads = grad_out[0].reshape(tok_rows, head_count, head_dim)
    grad_weighted = (grad_heads * head_factor[:, :, None]).astype(half)
    adjoint_local = jnp.einsum("thp,tn->hpn", grad_weighted, c_proj, preferred_element_type=fl)
    adjoint_all = lax.all_gather(adjoint_local, "tm")
    adjoint_in = jnp.zeros((head_count, head_dim, state_dim), fl)
    for k in range(n_blocks - 1, 0, -1):
        new = gate_all[k][:, None, None] * adjoint_in + adjoint_all[k]
        adjoint_in = jnp.where(k > my_block, new, adjoint_in)
    masked = decay_matrix(cum_decay) * step_size.T[:, None, :]
    scores = jnp.dot(c_proj, b_proj.T, preferred_element_type=fl)
    weights = (scores[None] * masked).astype(half)
    state_half = state_in.astype(half)
    adjoint_half = adjoint_in.astype(half)
    output = jnp.einsum("hts,shp->thp", weights, x_heads, preferred_element_type=fl)
    output = (
        output
        + jnp.einsum("tn,hpn->thp", c_proj, state_half, preferred_element_type=fl)
        * head_factor[:, :, None]
    )
    ssd_output = output.reshape(1, tok_rows, inner_width).astype(half)
    grad_x = jnp.einsum("hts,thp->shp", weights, grad_heads, preferred_element_type=fl)
    grad_x = (
        grad_x
        + jnp.einsum("sn,hpn->shp", b_proj, adjoint_half, preferred_element_type=fl)
        * tail_factor[:, :, None]
    )
    pair_scores = jnp.einsum("thp,shp->hts", grad_heads, x_heads, preferred_element_type=fl)
    pair_mixed = jnp.sum(pair_scores * masked, axis=0).astype(half)
    grad_b = jnp.dot(pair_mixed.T, c_proj, preferred_element_type=fl)
    grad_b = grad_b + jnp.einsum("shp,hpn->sn", x_weighted, adjoint_half, preferred_element_type=fl)
    grad_c = jnp.dot(pair_mixed, b_proj, preferred_element_type=fl)
    grad_c = grad_c + jnp.einsum(
        "thp,hpn->tn", grad_weighted, state_half, preferred_element_type=fl
    )
    grad_rows = jnp.concatenate(
        [
            grad_x.reshape(tok_rows, inner_width).astype(half),
            grad_b.astype(half),
            grad_c.astype(half),
        ],
        axis=1,
    )
    local_grad = jnp.einsum("tf,tw->fw", features, grad_rows, preferred_element_type=fl)
    share_grad = lax.psum_scatter(local_grad, "series", scatter_dimension=1, tiled=True)
    share_grad = lax.psum(share_grad, "tm")
    total_grad = lax.all_gather(share_grad, "series", axis=1, tiled=True)
    grad_in = total_grad / math.sqrt(series_count * seq_len)
    return (ssd_output, grad_in)


def solution(mesh):
    return jax.shard_map(
        on_device,
        mesh=mesh,
        in_specs=(P(None, ("tm", "series")), P(), P(), P(), P(), P(), P(), P("series", "tm", None)),
        out_specs=(P("series", "tm", None), P()),
        check_vma=False,
    )
```

profile of v0, /device:TPU:0, one launch (start us, length us, event | category | flops | bytes accessed | tf_op | source)
XLA Modules:
  0.0 243.4 jit_solution(498775291195324287)
XLA Ops:
  7.2 1.3 dynamic_slice.34
  9.8 44.0 %all-gather.1 = s32[32,16,8]{1,2,0:T(8,128)S(1)} all-gather(s32[1,16,8]{1,2,0:T(8,128)} %bitcast.172), channel_id=1, replica_groups=mesh['tm'=4,'series'=8] {'tm','series'}, dimensions={0}, use_global_device_ids=true | all-gather | bytes 16896 | tf_op jit(solution)/shard_map/all_gather | solution.py:30
  56.2 1.4 convert_reduce_fusion
  58.3 4.1 %fusion = f32[512,4]{0,1:T(4,128)S(1)} fusion(f32[4096]{0:T(1024)S(1)} %get-tuple-element.13, f32[4096]{0:T(1024)S(1)} %convert_element_type.97, f32[512]{0:T(512)S(1)} %bitcast.168, f32[4096,1]{0,1:T(1,128)S(1)} %bitcast.166, f32[4096,1]{0,1:T(1,128)S(1)} %bitcast.155, f32[4096,1]{0,1:T(1,128)S(1)} %bitcast.154, f32[4096,1]{0,1:T(1,128)S(1)} %sub.42), kind=kOutput, calls=%fused_computation.2 | convolution fusion | flops 107003904 | bytes 108544 | tf_op jit(solution)/shard_map/dot_general | solution.py:41
  62.5 1.6 convolution_convert_fusion
  64.2 1.1 compare_select_fusion
  66.2 1.2 reduce_window_sum.35
  68.9 1.5 copy.57
  71.1 2.0 copy.61
  73.2 1.1 fusion.24
  75.1 2.0 fusion.59
  77.4 1.6 slice.98
  79.6 3.2 %copy.54 = bf16[4,128,2048]{1,2,0:T(8,128)(2,1)S(1)} copy(bf16[4,128,2048]{2,1,0:T(8,128)(2,1)} %slice.98) | data formatting | bytes 4194304 | tf_op jit(solution)/shard_map/slice | solution.py:48
  82.8 1.2 exp.26
  84.0 1.7 exponential_multiply_fusion
  85.7 1.0 copy.60
  88.3 1.2 constant_dynamic-slice_fusion.1
  90.4 1.4 multiply_bitcast_fusion
  91.9 2.4 fusion.4
  96.3 2.3 convolution_bitcast_fusion
  99.3 3.6 %fusion.41 = f32[4,32,64,128]{3,2,1,0:T(8,128)} fusion(bf16[4,128,32,64]{1,3,2,0:T(8,128)(2,1)S(1)} %multiply_convert_fusion, bf16[4,128,2304]{2,1,0:T(8,128)(2,1)} %bitcast.143), kind=kOutput, calls=%fused_computation.67 | convolution fusion | flops 268435456 | bytes 6422528 | tf_op jit(solution)/shard_map/bthp,btn->bhpn/dot_general | solution.py:58
  102.9 23.4 %all-gather.7.cloned.1.call-done = f32[128,64,128]{2,1,0:T(8,128)} async-done(((f32[32,64,128]{2,1,0:T(8,128)}), f32[128,64,128]{2,1,0:T(8,128)}) %all-gather.7.cloned.1.call-update) | async-done | bytes 4194320 | tf_op jit(solution)/shard_map/all_gather | solution.py:79
  126.3 3.6 %fusion.15 = (bf16[1,32,64,128]{3,2,1,0:T(8,128)(2,1)S(1)}, bf16[1,32,64,128]{3,2,1,0:T(8,128)(2,1)S(1)}) fusion(f32[128,64,128]{2,1,0:T(8,128)} %all-gather.7.cloned.1.call-done, f32[32]{0:T(128)S(1)} %copy-done.19, f32[32]{0:T(128)S(1)} %copy-done.21, f32[32]{0:T(128)S(1)} %copy-done.22, pred[]{:T(512)S(6)} %lt.34, pred[]{:T(512)S(6)} %lt.33, pred[]{:T(512)S(6)} %lt.32, ...), kind=kLoop, calls=%fused_computation.30 | loop fusion | flops 4718592 | bytes 7340550 | tf_op jit(solution)/shard_map/convert_element_type | solution.py:88
  130.3 1.1 fusion.8
  131.8 1.6 fusion.25
  133.5 32.8 %reduce-scatter.2.cloned.1.call-done = f32[128,288]{0,1:T(8,128)} async-done(((f32[128,2304]{0,1:T(8,128)}), f32[128,288]{0,1:T(8,128)}) %reduce-scatter.2.cloned.1.call-update) | async-done | bytes 147472 | tf_op jit(solution)/shard_map/reduce_scatter | solution.py:119
  166.3 43.3 %all-reduce.2.cloned.1.call-done = f32[128,288]{0,1:T(8,128)} async-done(((f32[128,288]{0,1:T(8,128)}), f32[128,288]{0,1:T(8,128)}) %all-reduce.2.cloned.1.call-update) | async-done | bytes 147472 | tf_op jit(solution)/shard_map/psum | solution.py:120
  209.7 3.3 %convolution_bitcast_fusion.1 = f32[128,32,64]{0,2,1:T(8,128)S(1)} fusion(f32[32,128]{1,0:T(8,128)S(1)} %bitcast.165, f32[32,128]{1,0:T(8,128)S(1)} %bitcast.159, f32[128,128]{0,1:T(8,128)S(1)} %copy-done.13, pred[128,128]{0,1:T(8,128)(4,1)S(1)} %copy-done.17, bf16[4,128,32,64]{1,3,2,0:T(8,128)(2,1)} %bitcast.145, s32[]{:T(128)S(6)} %select_n.83), kind=kOutput, calls=%fused_computation.17 | convolution fusion | flops 70254592 | bytes 1703940 | tf_op jit(solution)/shard_map/hts,shp->thp/dot_general | solution.py:89
  213.0 1.1 fusion.7
  215.1 19.0 %all-gather.5.cloned.1.call-done = f32[128,2304]{0,1:T(8,128)} async-done(((f32[128,288]{0,1:T(8,128)}), f32[128,2304]{0,1:T(8,128)}) %all-gather.5.cloned.1.call-update) | async-done | bytes 1179664 | tf_op jit(solution)/shard_map/all_gather | solution.py:121
  234.1 1.3 broadcast_multiply_fusion
  235.5 1.4 copy.66
  (98 shorter events, 14.1 us)
Async XLA Ops:
  7.2 55.4 %copy-start = (bf16[128,2304]{1,0:T(8,128)(2,1)S(1)}, bf16[128,2304]{1,0:T(8,128)(2,1)}, u32[]{:S(2)}) copy-start(bf16[128,2304]{1,0:T(8,128)(2,1)} %param.11) | copy-start | bytes 1769476
  7.2 119.1 %all-gather.7.cloned.1.call-start = ((), (), s32[]{:S(2)}) async-start(), calls=%async_computation.4 | async-start | bytes 5242880 | tf_op jit(solution)/shard_map/all_gather | solution.py:79
  9.8 54.3 %copy-start.23 = (f32[128]{0:T(128)}, f32[128]{0:T(128)S(1)}, u32[]{:S(2)}) copy-start(f32[128]{0:T(128)S(1)} %add_multiply_fusion) | copy-start | bytes 1540
  62.4 1.7 copy-start.27
  62.5 1.7 copy-start.28
  62.5 3.0 %copy-start.25 = (f32[32]{0:T(128)S(1)}, f32[32]{0:T(128)}, u32[]{:S(2)}) copy-start(f32[32]{0:T(128)} %param.14) | copy-start | bytes 388
  62.5 2.8 %copy-start.18 = (f32[512,1]{0,1:T(1,128)}, f32[512,1]{0,1:T(1,128)S(1)}, u32[]{:S(2)}) copy-start(f32[512,1]{0,1:T(1,128)S(1)} %fusion.89) | copy-start | bytes 6148
  64.2 13.2 %copy-start.1 = (bf16[512,2304]{1,0:T(8,128)(2,1)}, bf16[512,2304]{1,0:T(8,128)(2,1)S(1)}, u32[]{:S(2)}) copy-start(bf16[512,2304]{1,0:T(8,128)(2,1)S(1)} %convolution_convert_fusion) | copy-start | bytes 7077892
  67.4 11.6 %copy-start.7 = (f32[4,128,32]{2,1,0:T(8,128)}, f32[4,128,32]{2,1,0:T(8,128)S(1)}, u32[]{:S(2)}) copy-start(f32[4,128,32]{2,1,0:T(8,128)S(1)} %reduce_window_sum.35) | copy-start | bytes 196612
  77.1 89.1 %reduce-scatter.2.cloned.1.call-start = ((), (), s32[]{:S(2)}) async-start(), calls=%async_computation.1 | async-start | bytes 1327104 | tf_op jit(solution)/shard_map/reduce_scatter | solution.py:119
  79.6 12.3 %copy-start.6 = (bf16[1,128,2048]{1,2,0:T(8,128)(2,1)S(1)}, bf16[1,128,2048]{1,2,0:T(8,128)(2,1)}, u32[]{:S(2)}) copy-start(bf16[1,128,2048]{1,2,0:T(8,128)(2,1)} %copy.61) | copy-start | bytes 1572868
  82.8 11.5 %copy-start.2 = (bf16[4,128,2048]{1,2,0:T(8,128)(2,1)}, bf16[4,128,2048]{1,2,0:T(8,128)(2,1)S(1)}, u32[]{:S(2)}) copy-start(bf16[4,128,2048]{1,2,0:T(8,128)(2,1)S(1)} %copy.54) | copy-start | bytes 6291460
  89.5 6.7 %copy-start.14 = (f32[1,128,32]{1,0,2:T(1,128)}, f32[1,128,32]{1,0,2:T(1,128)S(1)}, u32[]{:S(2)}) copy-start(f32[1,128,32]{1,0,2:T(1,128)S(1)} %constant_dynamic-slice_fusion.2) | copy-start | bytes 49156
  89.5 6.7 %copy-start.16 = (pred[128,128]{0,1:T(8,128)(4,1)}, pred[128,128]{0,1:T(8,128)(4,1)S(1)}, u32[]{:S(2)}) copy-start(pred[128,128]{0,1:T(8,128)(4,1)S(1)} %iota_compare_fusion) | copy-start | bytes 49156
  90.4 5.8 %copy-start.12 = (f32[128,128]{0,1:T(8,128)}, f32[128,128]{0,1:T(8,128)S(1)}, u32[]{:S(2)}) copy-start(f32[128,128]{0,1:T(8,128)S(1)} %fusion.64) | copy-start | bytes 196612
  91.9 4.4 %copy-start.10 = (f32[1,128,32]{1,2,0:T(8,128)S(1)}, f32[1,128,32]{1,2,0:T(8,128)}, u32[]{:S(2)}) copy-start(f32[1,128,32]{1,2,0:T(8,128)} %copy.57) | copy-start | bytes 49156
  96.3 2.4 copy-start.3
  99.3 27.0 %copy-start.19 = (f32[32]{0:T(128)S(1)}, f32[32]{0:T(128)}, u32[]{:S(2)}) copy-start(f32[32]{0:T(128)} %get-tuple-element.14) | copy-start | bytes 388
  99.3 27.0 %copy-start.20 = (f32[32]{0:T(128)S(1)}, f32[32]{0:T(128)}, u32[]{:S(2)}) copy-start(f32[32]{0:T(128)} %get-tuple-element.15) | copy-start | bytes 388
  99.3 27.0 %copy-start.21 = (f32[32]{0:T(128)S(1)}, f32[32]{0:T(128)}, u32[]{:S(2)}) copy-start(f32[32]{0:T(128)} %get-tuple-element.16) | copy-start | bytes 388
  99.3 27.0 %copy-start.22 = (f32[32]{0:T(128)S(1)}, f32[32]{0:T(128)}, u32[]{:S(2)}) copy-start(f32[32]{0:T(128)} %get-tuple-element.17) | copy-start | bytes 388
  126.3 4.0 %copy-start.8 = (f32[128,32,64]{0,2,1:T(8,128)S(1)}, f32[128,32,64]{0,2,1:T(8,128)}, u32[]{:S(2)}) copy-start(f32[128,32,64]{0,2,1:T(8,128)} %convolution_bitcast_fusion) | copy-start | bytes 3145732
  126.3 4.0 %copy-start.9 = (f32[1,128,32]{1,2,0:T(8,128)S(1)}, f32[1,128,32]{1,2,0:T(8,128)}, u32[]{:S(2)}) copy-start(f32[1,128,32]{1,2,0:T(8,128)} %copy.64) | copy-start | bytes 49156
  129.9 1.5 copy-start.5
  129.9 1.9 copy-start.24
  129.9 1.9 copy-start.26
  131.4 78.3 %copy-start.11 = (f32[1,128,32]{1,2,0:T(8,128)S(1)}, f32[1,128,32]{1,2,0:T(8,128)}, u32[]{:S(2)}) copy-start(f32[1,128,32]{1,2,0:T(8,128)} %copy.57) | copy-start | bytes 49156
  131.4 78.3 %copy-start.13 = (f32[128,128]{0,1:T(8,128)S(1)}, f32[128,128]{0,1:T(8,128)}, u32[]{:S(2)}) copy-start(f32[128,128]{0,1:T(8,128)} %copy-done.12) | copy-start | bytes 196612
  131.4 78.3 %copy-start.15 = (f32[1,128,32]{1,0,2:T(1,128)S(1)}, f32[1,128,32]{1,0,2:T(1,128)}, u32[]{:S(2)}) copy-start(f32[1,128,32]{1,0,2:T(1,128)} %copy-done.14) | copy-start | bytes 49156
  131.4 78.3 %copy-start.17 = (pred[128,128]{0,1:T(8,128)(4,1)S(1)}, pred[128,128]{0,1:T(8,128)(4,1)}, u32[]{:S(2)}) copy-start(pred[128,128]{0,1:T(8,128)(4,1)} %copy-done.16) | copy-start | bytes 49156
  133.4 76.2 %all-reduce.2.cloned.1.call-start = ((), (), s32[]{:S(2)}) async-start(), calls=%async_computation.2 | async-start | bytes 294912 | tf_op jit(solution)/shard_map/psum | solution.py:120
  166.3 67.8 %all-gather.5.cloned.1.call-start = ((), (), s32[]{:S(2)}) async-start(), calls=%async_computation.3 | async-start | bytes 1327104 | tf_op jit(solution)/shard_map/all_gather | solution.py:121
  (1 other events, 0.8 us)
Sparse Core Ops, SparseCore 0:
  77.3 48.9 all-gather.6
  133.6 32.6 reduce-scatter.1
  169.2 40.4 all-reduce.1
  211.3 22.8 all-gather.4
where the time goes:
time: 245 us; the launch traced here: 243 us
  waiting for transfers between devices  119 us (49%)
  blocking collectives  44 us (18%)
  matrix products  27.7 us (11%)
  local copies, waits for them, and re-layouts  21.2 us (9%)
  between operations  16.2 us (7%)
  other arithmetic  15.3 us (6%)
    all_gather x1, blocking collectives, on_device(): all_codes = lax.all_gather(codes, ('tm', 'series'), axis=1, tiled=True)  44 us
    psum x1, waiting for transfers between devices, on_device(): share_grad = lax.psum(share_grad, 'tm')  43.3 us
    reduce_scatter x1, waiting for transfers between devices, on_device(): lax.psum_scatter(local_grad, 'series', scatter_dimension=1, tiled=True)  32.8 us
    all_gather x1, waiting for transfers between devices, on_device(): adjoint_all = lax.all_gather(adjoint_local, 'tm')  23.4 us
    all_gather x1, waiting for transfers between devices, on_device(): total_grad = lax.all_gather(share_grad, 'series', axis=1, tiled=True)  19 us
    unnamed x62, local copies, waits for them, and re-layouts  5.44 us
  transfers between devices with their start and end apart: 4, of which 4 were waited for; matrix products, arithmetic and copies ran while one was open for 13% of the time, Pallas kernels for 0%

commit v1 on v0

--- a/solution.py
+++ b/solution.py
@@ -27,7 +27,14 @@
     series_count = lax.axis_size("series")
     my_block = lax.axis_index("tm")
     my_series = lax.axis_index("series")
-    all_codes = lax.all_gather(codes, ("tm", "series"), axis=1, tiled=True)
+    ways, here = (lax.axis_size(("tm", "series")), lax.axis_index(("tm", "series")))
+    all_codes, reach = (codes, 1)
+    while reach < ways:
+        theirs = lax.ppermute(all_codes, ("tm", "series"), [(d, d ^ reach) for d in range(ways)])
+        mine_first = jnp.concatenate([all_codes, theirs], axis=1)
+        theirs_first = jnp.concatenate([theirs, all_codes], axis=1)
+        all_codes = jnp.where(here & reach == 0, mine_first, theirs_first)
+        reach = 2 * reach
     row = lax.dynamic_index_in_dim(all_codes, owner_slot[my_series], axis=0, keepdims=False)
     reading = row.astype(fl)
     edge_float = edges.astype(fl)

time: 245 us -> 220 us (0.90)
  blocking collectives: 44 us -> 0 us
  starting transfers between devices: 0.34 us -> 10.5 us
  waiting for transfers between devices: 119 us -> 126 us
    all_gather x1 -> x0, blocking collectives: 44 us -> none  [on_device(): all_codes = lax.all_gather(codes, ('tm', 'series'), axis=1, tiled=True)]
    ppermute x0 -> x5, starting transfers between devices: none -> 10.1 us  [on_device(): lax.ppermute(all_codes, ('tm', 'series'), [(d, d ^ reach) for d in range(...]
    ppermute x0 -> x5, waiting for transfers between devices: none -> 4.41 us  [on_device(): lax.ppermute(all_codes, ('tm', 'series'), [(d, d ^ reach) for d in range(...]
    all_gather x1, waiting for transfers between devices: 23.4 us -> 26.6 us  [on_device(): adjoint_all = lax.all_gather(adjoint_local, 'tm')]
    unnamed x62 -> x61, local copies, waits for them, and re-layouts: 5.44 us -> 5.35 us
  transfers between devices with their start and end apart: 4 -> 9, of which waited for: 4 -> 8; matrix products, arithmetic and copies ran while one was open for 13% -> 17% of each run, Pallas kernels for 0% -> 0%
where the time goes in v1:
time: 220 us; the launch traced here: 219 us
  waiting for transfers between devices  126 us (57%)
  matrix products  27.8 us (13%)
  local copies, waits for them, and re-layouts  21.1 us (10%)
  other arithmetic  17 us (8%)
  between operations  16.2 us (7%)
  starting transfers between devices  10.5 us (5%)
    psum x1, waiting for transfers between devices, on_device(): share_grad = lax.psum(share_grad, 'tm')  43.2 us
    reduce_scatter x1, waiting for transfers between devices, on_device(): lax.psum_scatter(local_grad, 'series', scatter_dimension=1, tiled=True)  32.9 us
    all_gather x1, waiting for transfers between devices, on_device(): adjoint_all = lax.all_gather(adjoint_local, 'tm')  26.6 us
    all_gather x1, waiting for transfers between devices, on_device(): total_grad = lax.all_gather(share_grad, 'series', axis=1, tiled=True)  19 us
    ppermute x5, starting transfers between devices, on_device(): lax.ppermute(all_codes, ('tm', 'series'), [(d, d ^ reach) for d in range(...  10.1 us
    unnamed x61, local copies, waits for them, and re-layouts  5.35 us
    dynamic_slice x6, local copies, waits for them, and re-layouts, mine(): return lax.dynamic_index_in_dim(a, my_block, axis=0, keepdims=False)  4.94 us
    slice x2, local copies, waits for them, and re-layouts, on_device(): projected_all[:, :, :inner_width]  4.74 us
  transfers between devices with their start and end apart: 9, of which 8 were waited for; matrix products, arithmetic and copies ran while one was open for 17% of the time, Pallas kernels for 0%

profile of v1, /device:TPU:0, one launch (start us, length us, event | category | flops | bytes accessed | tf_op | source)
XLA Modules:
  0.0 218.7 jit_solution(3124431067188828443)
XLA Ops:
  9.6 2.9 %collective-permute-start.1 = (s32[8,32]{1,0:T(8,128)S(1)}, s32[8,32]{1,0:T(8,128)S(1)}, u32[]{:S(2)}, u32[]{:S(2)}) collective-permute-start(s32[8,32]{1,0:T(8,128)S(1)} %add_select_fusion.1), channel_id=1, source_target_pairs={{0,2},{1,3},{2,0},{3,1},{4,6},{5,7},{6,4},{7,5},{8,10},{9,11},{10,... | collective-permute-start | bytes 3080 | tf_op jit(solution)/shard_map/ppermute | solution.py:33
  12.5 1.6 collective-permute-done.1
  14.2 3.0 %collective-permute-start.2 = (s32[8,64]{1,0:T(8,128)S(1)}, s32[8,64]{1,0:T(8,128)S(1)}, u32[]{:S(2)}, u32[]{:S(2)}) collective-permute-start(s32[8,64]{1,0:T(8,128)S(1)} %add_select_fusion.2), channel_id=1, source_target_pairs={{0,4},{1,5},{2,6},{3,7},{4,0},{5,1},{6,2},{7,3},{8,12},{9,13},{10,... | collective-permute-start | bytes 6152 | tf_op jit(solution)/shard_map/ppermute | solution.py:33
  18.9 1.8 collective-permute-start.3
  22.5 1.8 collective-permute-start.4
  24.4 1.2 dynamic_slice.34
  26.9 2.0 copy.57
  29.6 1.4 convert_reduce_fusion
  31.7 4.1 %fusion = f32[512,4]{0,1:T(4,128)S(1)} fusion(f32[4096]{0:T(1024)S(1)} %get-tuple-element.13, f32[4096]{0:T(1024)S(1)} %convert_element_type.97, f32[512]{0:T(512)S(1)} %bitcast.163, f32[4096,1]{0,1:T(1,128)S(1)} %bitcast.167, f32[4096,1]{0,1:T(1,128)S(1)} %bitcast.154, f32[4096,1]{0,1:T(1,128)S(1)} %bitcast.153, f32[4096,1]{0,1:T(1,128)S(1)} %sub.42), kind=kOutput, calls=%fused_computation.2 | convolution fusion | flops 107003904 | bytes 108544 | tf_op jit(solution)/shard_map/dot_general | solution.py:48
  36.0 1.6 convolution_convert_fusion
  39.6 1.2 reduce_window_sum.35
  42.3 1.5 copy.53
  44.5 1.1 fusion.24
  46.5 2.0 fusion.59
  49.4 1.6 slice.98
  51.6 3.1 %copy.50 = bf16[4,128,2048]{1,2,0:T(8,128)(2,1)S(1)} copy(bf16[4,128,2048]{2,1,0:T(8,128)(2,1)} %slice.98) | data formatting | bytes 4194304 | tf_op jit(solution)/shard_map/slice | solution.py:55
  54.7 1.3 exp.26
  56.0 1.7 exponential_multiply_fusion
  60.3 1.2 constant_dynamic-slice_fusion.1
  62.5 1.4 multiply_bitcast_fusion
  64.0 2.4 %fusion.4 = bf16[128,128]{0,1:T(8,128)(2,1)S(1)} fusion(bf16[128,32,64]{0,2,1:T(8,128)(2,1)S(1)} %bitcast.149, f32[32,128]{1,0:T(8,128)S(1)} %bitcast.164, f32[32,128]{1,0:T(8,128)} %bitcast.156, pred[128,128]{0,1:T(8,128)(4,1)} %iota_compare_fusion, bf16[4,128,32,64]{1,3,2,0:T(8,128)(2,1)S(1)} %bitcast.143, s32[]{:T(128)S(6)} %select_n.133), kind=kOutput, calls=%fused_computation.9 | convolution fusion | flops 70238208 | bytes 1146884 | tf_op jit(solution)/shard_map/thp,shp->hts/dot_general | solution.py:109
  68.4 2.4 %convolution_bitcast_fusion = f32[128,32,64]{0,2,1:T(8,128)} fusion(bf16[128,32,64]{0,2,1:T(8,128)(2,1)S(1)} %bitcast.150, f32[32,128]{1,0:T(8,128)S(1)} %bitcast.165, f32[32,128]{1,0:T(8,128)S(1)} %bitcast.157, f32[128,128]{0,1:T(8,128)S(1)} %fusion.64, pred[128,128]{0,1:T(8,128)(4,1)S(1)} %copy-done.14), kind=kOutput, calls=%fused_computation.14 | convolution fusion | flops 70254592 | bytes 1687552 | tf_op jit(solution)/shard_map/hts,thp->shp/dot_general | solution.py:103
  71.5 3.6 %fusion.41 = f32[4,32,64,128]{3,2,1,0:T(8,128)} fusion(bf16[4,128,32,64]{1,3,2,0:T(8,128)(2,1)S(1)} %multiply_convert_fusion, bf16[4,128,2304]{2,1,0:T(8,128)(2,1)} %bitcast.142), kind=kOutput, calls=%fused_computation.67 | convolution fusion | flops 268435456 | bytes 6422528 | tf_op jit(solution)/shard_map/bthp,btn->bhpn/dot_general | solution.py:65
  75.1 26.6 %all-gather.6.cloned.1.call-done = f32[128,64,128]{2,1,0:T(8,128)} async-done(((f32[32,64,128]{2,1,0:T(8,128)}), f32[128,64,128]{2,1,0:T(8,128)}) %all-gather.6.cloned.1.call-update) | async-done | bytes 4194320 | tf_op jit(solution)/shard_map/all_gather | solution.py:86
  101.7 3.6 %fusion.15 = (bf16[1,32,64,128]{3,2,1,0:T(8,128)(2,1)S(1)}, bf16[1,32,64,128]{3,2,1,0:T(8,128)(2,1)S(1)}) fusion(f32[128,64,128]{2,1,0:T(8,128)} %all-gather.6.cloned.1.call-done, f32[32]{0:T(128)S(1)} %copy-done.19, f32[32]{0:T(128)S(1)} %copy-done.21, f32[32]{0:T(128)S(1)} %copy-done.22, pred[]{:T(512)S(6)} %lt.34, pred[]{:T(512)S(6)} %lt.33, pred[]{:T(512)S(6)} %lt.32, ...), kind=kLoop, calls=%fused_computation.30 | loop fusion | flops 4718592 | bytes 7340550 | tf_op jit(solution)/shard_map/convert_element_type | solution.py:95
  107.2 1.6 fusion.25
  108.9 32.9 %reduce-scatter.2.cloned.1.call-done = f32[128,288]{0,1:T(8,128)} async-done(((f32[128,2304]{0,1:T(8,128)}), f32[128,288]{0,1:T(8,128)}) %reduce-scatter.2.cloned.1.call-update) | async-done | bytes 147472 | tf_op jit(solution)/shard_map/reduce_scatter | solution.py:126
  141.8 43.2 %all-reduce.2.cloned.1.call-done = f32[128,288]{0,1:T(8,128)} async-done(((f32[128,288]{0,1:T(8,128)}), f32[128,288]{0,1:T(8,128)}) %all-reduce.2.cloned.1.call-update) | async-done | bytes 147472 | tf_op jit(solution)/shard_map/psum | solution.py:127
  185.1 3.3 %convolution_bitcast_fusion.1 = f32[128,32,64]{0,2,1:T(8,128)S(1)} fusion(f32[32,128]{1,0:T(8,128)S(1)} %bitcast.166, f32[32,128]{1,0:T(8,128)S(1)} %bitcast.158, f32[128,128]{0,1:T(8,128)S(1)} %copy-done.13, pred[128,128]{0,1:T(8,128)(4,1)S(1)} %copy-done.15, bf16[4,128,32,64]{1,3,2,0:T(8,128)(2,1)} %bitcast.144, s32[]{:T(128)S(6)} %select_n.133), kind=kOutput, calls=%fused_computation.17 | convolution fusion | flops 70254592 | bytes 1703940 | tf_op jit(solution)/shard_map/hts,shp->thp/dot_general | solution.py:96
  190.4 19.0 %all-gather.4.cloned.1.call-done = f32[128,2304]{0,1:T(8,128)} async-done(((f32[128,288]{0,1:T(8,128)}), f32[128,2304]{0,1:T(8,128)}) %all-gather.4.cloned.1.call-update) | async-done | bytes 1179664 | tf_op jit(solution)/shard_map/all_gather | solution.py:128
  209.5 1.3 broadcast_multiply_fusion
  210.8 1.4 copy.62
  (109 shorter events, 23.2 us)
Async XLA Ops:
  7.2 28.8 %copy-start = (bf16[128,2304]{1,0:T(8,128)(2,1)S(1)}, bf16[128,2304]{1,0:T(8,128)(2,1)}, u32[]{:S(2)}) copy-start(bf16[128,2304]{1,0:T(8,128)(2,1)} %param.11) | copy-start | bytes 1769476
  7.2 94.5 %all-gather.6.cloned.1.call-start = ((), (), s32[]{:S(2)}) async-start(), calls=%async_computation.4 | async-start | bytes 5242880 | tf_op jit(solution)/shard_map/all_gather | solution.py:86
  7.2 1.6 collective-permute-start
  9.6 4.5 %collective-permute-start.1 = (s32[8,32]{1,0:T(8,128)S(1)}, s32[8,32]{1,0:T(8,128)S(1)}, u32[]{:S(2)}, u32[]{:S(2)}) collective-permute-start(s32[8,32]{1,0:T(8,128)S(1)} %add_select_fusion.1), channel_id=1, source_target_pairs={{0,2},{1,3},{2,0},{3,1},{4,6},{5,7},{6,4},{7,5},{8,10},{9,11},{10,... | collective-permute-start | bytes 3080 | tf_op jit(solution)/shard_map/ppermute | solution.py:33
  14.2 4.6 %collective-permute-start.2 = (s32[8,64]{1,0:T(8,128)S(1)}, s32[8,64]{1,0:T(8,128)S(1)}, u32[]{:S(2)}, u32[]{:S(2)}) collective-permute-start(s32[8,64]{1,0:T(8,128)S(1)} %add_select_fusion.2), channel_id=1, source_target_pairs={{0,4},{1,5},{2,6},{3,7},{4,0},{5,1},{6,2},{7,3},{8,12},{9,13},{10,... | collective-permute-start | bytes 6152 | tf_op jit(solution)/shard_map/ppermute | solution.py:33
  18.9 3.6 %collective-permute-start.3 = (s32[8,128]{1,0:T(8,128)S(1)}, s32[8,128]{1,0:T(8,128)S(1)}, u32[]{:S(2)}, u32[]{:S(2)}) collective-permute-start(s32[8,128]{1,0:T(8,128)S(1)} %add_select_fusion.3), channel_id=1, source_target_pairs={{0,8},{1,9},{2,10},{3,11},{4,12},{5,13},{6,14},{7,15},{8,0},{9,1},... | collective-permute-start | bytes 12296 | tf_op jit(solution)/shard_map/ppermute | solution.py:33
  22.5 7.1 %collective-permute-start.4 = (s32[8,256]{1,0:T(8,128)S(1)}, s32[8,256]{1,0:T(8,128)S(1)}, u32[]{:S(2)}, u32[]{:S(2)}) collective-permute-start(s32[8,256]{1,0:T(8,128)S(1)} %add_select_fusion), channel_id=1, source_target_pairs={{0,16},{1,17},{2,18},{3,19},{4,20},{5,21},{6,22},{7,23},{8,24},{9,... | collective-permute-start | bytes 24584 | tf_op jit(solution)/shard_map/ppermute | solution.py:33
  24.4 13.2 %copy-start.23 = (f32[128]{0:T(128)}, f32[128]{0:T(128)S(1)}, u32[]{:S(2)}) copy-start(f32[128]{0:T(128)S(1)} %add_multiply_fusion) | copy-start | bytes 1540
  35.9 3.0 %copy-start.25 = (f32[32]{0:T(128)S(1)}, f32[32]{0:T(128)}, u32[]{:S(2)}) copy-start(f32[32]{0:T(128)} %param.14) | copy-start | bytes 388
  35.9 2.8 %copy-start.18 = (f32[512,1]{0,1:T(1,128)}, f32[512,1]{0,1:T(1,128)S(1)}, u32[]{:S(2)}) copy-start(f32[512,1]{0,1:T(1,128)S(1)} %fusion.91) | copy-start | bytes 6148
  37.6 11.8 %copy-start.1 = (bf16[512,2304]{1,0:T(8,128)(2,1)}, bf16[512,2304]{1,0:T(8,128)(2,1)S(1)}, u32[]{:S(2)}) copy-start(bf16[512,2304]{1,0:T(8,128)(2,1)S(1)} %convolution_convert_fusion) | copy-start | bytes 7077892
  40.9 10.2 %copy-start.7 = (f32[4,128,32]{2,1,0:T(8,128)}, f32[4,128,32]{2,1,0:T(8,128)S(1)}, u32[]{:S(2)}) copy-start(f32[4,128,32]{2,1,0:T(8,128)S(1)} %reduce_window_sum.35) | copy-start | bytes 196612
  48.5 93.2 %reduce-scatter.2.cloned.1.call-start = ((), (), s32[]{:S(2)}) async-start(), calls=%async_computation.1 | async-start | bytes 1327104 | tf_op jit(solution)/shard_map/reduce_scatter | solution.py:126
  51.6 12.4 %copy-start.6 = (bf16[1,128,2048]{1,2,0:T(8,128)(2,1)S(1)}, bf16[1,128,2048]{1,2,0:T(8,128)(2,1)}, u32[]{:S(2)}) copy-start(bf16[1,128,2048]{1,2,0:T(8,128)(2,1)} %copy.57) | copy-start | bytes 1572868
  54.7 11.7 %copy-start.2 = (bf16[4,128,2048]{1,2,0:T(8,128)(2,1)}, bf16[4,128,2048]{1,2,0:T(8,128)(2,1)S(1)}, u32[]{:S(2)}) copy-start(bf16[4,128,2048]{1,2,0:T(8,128)(2,1)S(1)} %copy.50) | copy-start | bytes 6291460
  61.6 6.7 %copy-start.16 = (f32[1,128,32]{1,0,2:T(1,128)}, f32[1,128,32]{1,0,2:T(1,128)S(1)}, u32[]{:S(2)}) copy-start(f32[1,128,32]{1,0,2:T(1,128)S(1)} %constant_dynamic-slice_fusion.2) | copy-start | bytes 49156
  62.5 5.8 %copy-start.12 = (f32[128,128]{0,1:T(8,128)}, f32[128,128]{0,1:T(8,128)S(1)}, u32[]{:S(2)}) copy-start(f32[128,128]{0,1:T(8,128)S(1)} %fusion.64) | copy-start | bytes 196612
  64.0 4.4 %copy-start.10 = (f32[1,128,32]{1,2,0:T(8,128)S(1)}, f32[1,128,32]{1,2,0:T(8,128)}, u32[]{:S(2)}) copy-start(f32[1,128,32]{1,2,0:T(8,128)} %copy.53) | copy-start | bytes 49156
  64.0 4.4 %copy-start.14 = (pred[128,128]{0,1:T(8,128)(4,1)S(1)}, pred[128,128]{0,1:T(8,128)(4,1)}, u32[]{:S(2)}) copy-start(pred[128,128]{0,1:T(8,128)(4,1)} %iota_compare_fusion) | copy-start | bytes 49156
  68.4 2.4 %copy-start.3 = (bf16[4,128,2048]{1,2,0:T(8,128)(2,1)S(1)}, bf16[4,128,2048]{1,2,0:T(8,128)(2,1)}, u32[]{:S(2)}) copy-start(bf16[4,128,2048]{1,2,0:T(8,128)(2,1)} %copy-done.2) | copy-start | bytes 6291460
  71.4 30.2 %copy-start.19 = (f32[32]{0:T(128)S(1)}, f32[32]{0:T(128)}, u32[]{:S(2)}) copy-start(f32[32]{0:T(128)} %get-tuple-element.14) | copy-start | bytes 388
  71.4 30.2 %copy-start.20 = (f32[32]{0:T(128)S(1)}, f32[32]{0:T(128)}, u32[]{:S(2)}) copy-start(f32[32]{0:T(128)} %get-tuple-element.15) | copy-start | bytes 388
  71.5 30.2 %copy-start.21 = (f32[32]{0:T(128)S(1)}, f32[32]{0:T(128)}, u32[]{:S(2)}) copy-start(f32[32]{0:T(128)} %get-tuple-element.16) | copy-start | bytes 388
  71.5 30.2 %copy-start.22 = (f32[32]{0:T(128)S(1)}, f32[32]{0:T(128)}, u32[]{:S(2)}) copy-start(f32[32]{0:T(128)} %get-tuple-element.17) | copy-start | bytes 388
  101.7 4.0 %copy-start.8 = (f32[128,32,64]{0,2,1:T(8,128)S(1)}, f32[128,32,64]{0,2,1:T(8,128)}, u32[]{:S(2)}) copy-start(f32[128,32,64]{0,2,1:T(8,128)} %convolution_bitcast_fusion) | copy-start | bytes 3145732
  101.7 4.0 %copy-start.9 = (f32[1,128,32]{1,2,0:T(8,128)S(1)}, f32[1,128,32]{1,2,0:T(8,128)}, u32[]{:S(2)}) copy-start(f32[1,128,32]{1,2,0:T(8,128)} %copy.60) | copy-start | bytes 49156
  106.8 78.3 %copy-start.11 = (f32[1,128,32]{1,2,0:T(8,128)S(1)}, f32[1,128,32]{1,2,0:T(8,128)}, u32[]{:S(2)}) copy-start(f32[1,128,32]{1,2,0:T(8,128)} %copy.53) | copy-start | bytes 49156
  106.8 78.3 %copy-start.13 = (f32[128,128]{0,1:T(8,128)S(1)}, f32[128,128]{0,1:T(8,128)}, u32[]{:S(2)}) copy-start(f32[128,128]{0,1:T(8,128)} %copy-done.12) | copy-start | bytes 196612
  106.8 78.3 %copy-start.15 = (pred[128,128]{0,1:T(8,128)(4,1)S(1)}, pred[128,128]{0,1:T(8,128)(4,1)}, u32[]{:S(2)}) copy-start(pred[128,128]{0,1:T(8,128)(4,1)} %iota_compare_fusion) | copy-start | bytes 49156
  106.8 78.3 %copy-start.17 = (f32[1,128,32]{1,0,2:T(1,128)S(1)}, f32[1,128,32]{1,0,2:T(1,128)}, u32[]{:S(2)}) copy-start(f32[1,128,32]{1,0,2:T(1,128)} %copy-done.16) | copy-start | bytes 49156
  108.8 76.2 %all-reduce.2.cloned.1.call-start = ((), (), s32[]{:S(2)}) async-start(), calls=%async_computation.2 | async-start | bytes 294912 | tf_op jit(solution)/shard_map/psum | solution.py:127
  141.8 67.7 %all-gather.4.cloned.1.call-start = ((), (), s32[]{:S(2)}) async-start(), calls=%async_computation.3 | async-start | bytes 1327104 | tf_op jit(solution)/shard_map/all_gather | solution.py:128
  (6 other events, 9.5 us)
Sparse Core Ops, SparseCore 0:
  48.6 52.9 all-gather.5
  108.9 32.7 reduce-scatter.1
  144.7 40.2 all-reduce.1
  186.6 22.8 all-gather.3
